TPU v7x, 256 devices: a whole 4x4x8 slice. The times are simulated.
256 devices in a mesh: rows: 32 (over y, z), grp: 8 (over x, core).
Axes of the slice: x: 4, y: 4, z: 8, core: 2. Of those that a mesh axis runs over, the one named last changes fastest.
Arguments:
- item_table: bfloat16 [507904, 128], P(('rows', 'grp'))
- histories: int32 [16384, 64], P(('rows', 'grp')), may hold values from 0 to 507903, as said below
- counts: int32 [16384], P(('rows', 'grp')), may hold values from 32 to 64
Outputs:
- user_vectors: float32 [16384, 128], P(('rows', 'grp'))
- item_rhs: float32 [507904, 128], P(('rows', 'grp'))
Inputs may be any that keep to these rules, and one draw needn't show every extreme that they name: `histories`: entry j of user u is used only if j < counts[u]. The used entries of the users of one device name items of one owner (rows o * 1984 to (o + 1) * 1984 - 1) at most 32 times, and in every draw some owner is named exactly 32 times by the used entries of every device.
All inputs are finite; a program needn't handle non-finite values.
Results may differ from a plain program's by a relative error of at most 0.0064.
Values may be sent and summed in bfloat16 or wider, within the bound.
No kernel may reach another device: no remote copies, remote signals or barrier semaphores. Data moves between devices by JAX's collectives and lax.ppermute only.
A program may use at most 64 MiB of HBM per device.

v0:
```python
import jax
import jax.numpy as jnp
from jax import lax
from jax.sharding import PartitionSpec as P

ITERS = 3
unobserved_weight = 25.0
ridge = 0.1


def on_device(item_table, histories, counts):
    row_count = lax.axis_size("rows")
    group_count = lax.axis_size("grp")
    devices = row_count * group_count
    table_rows, embed_width = item_table.shape
    user_count, history_length = histories.shape
    lookups = user_count * history_length
    capacity = max(4, 2 * lookups // devices)
    slots_total = devices * capacity
    local_gram = lax.dot_general(
        item_table, item_table, (((0,), (0,)), ((), ())), preferred_element_type=jnp.float32
    )
    gramian = lax.psum(local_gram, ("rows", "grp"))
    positions = lax.broadcasted_iota(jnp.int32, (user_count, history_length), 1)
    live = positions < counts[:, None]
    weights = live.astype(jnp.float32)
    flat_ids = histories.reshape(-1)
    owners = flat_ids // table_rows
    local_rows = flat_ids - owners * table_rows
    owner_key = jnp.where(live.reshape(-1), owners, devices)
    ordering = jnp.argsort(owner_key, stable=True)
    sorted_key = owner_key[ordering]
    starts = jnp.searchsorted(sorted_key, jnp.arange(devices + 1, dtype=jnp.int32), side="left")
    ranks = jnp.arange(lookups, dtype=jnp.int32) - starts[sorted_key]
    sorted_slots = jnp.where(sorted_key < devices, sorted_key * capacity + ranks, slots_total)
    slot_index = jnp.zeros((lookups,), jnp.int32).at[ordering].set(sorted_slots)
    requests = (
        jnp.full((slots_total,), table_rows, jnp.int32).at[slot_index].set(local_rows, mode="drop")
    )
    requests = requests.reshape(row_count, group_count, capacity)
    incoming = lax.all_to_all(
        lax.all_to_all(requests, "grp", split_axis=1, concat_axis=1, tiled=True),
        "rows",
        split_axis=0,
        concat_axis=0,
        tiled=True,
    )
    answered = item_table[jnp.minimum(incoming, table_rows - 1)]
    replies = lax.all_to_all(
        lax.all_to_all(answered, "grp", split_axis=1, concat_axis=1, tiled=True),
        "rows",
        split_axis=0,
        concat_axis=0,
        tiled=True,
    )
    reply_rows = replies.reshape(slots_total, embed_width)
    fetched = reply_rows[jnp.minimum(slot_index, slots_total - 1)].reshape(
        user_count, history_length, embed_width
    )
    narrow_weights = weights.astype(jnp.bfloat16)
    target = jnp.einsum("ul,ulk->uk", narrow_weights, fetched, preferred_element_type=jnp.float32)
    unseen_scale = unobserved_weight / (table_rows * devices)
    solution = jnp.zeros_like(target)
    residual = target
    direction = target
    norm_now = jnp.sum(residual * residual, axis=1)
    for iteration in range(ITERS):
        narrow = direction.astype(jnp.bfloat16)
        scores = jnp.einsum("ulk,uk->ul", fetched, narrow, preferred_element_type=jnp.float32)
        scores = (scores * weights).astype(jnp.bfloat16)
        returned = jnp.einsum("ulk,ul->uk", fetched, scores, preferred_element_type=jnp.float32)
        curved = jnp.dot(direction, gramian, precision=lax.Precision.HIGHEST)
        applied = unseen_scale * curved + returned + ridge * direction
        step_size = norm_now / jnp.sum(direction * applied, axis=1)
        solution = solution + step_size[:, None] * direction
        residual = residual - step_size[:, None] * applied
        norm_next = jnp.sum(residual * residual, axis=1)
        direction = residual + (norm_next / norm_now)[:, None] * direction
        norm_now = norm_next
    repeated = jnp.repeat(solution, history_length, axis=0)
    partials = (
        jnp.zeros((slots_total, embed_width), jnp.float32).at[slot_index].set(repeated, mode="drop")
    )
    partials = partials.reshape(row_count, group_count, capacity, embed_width)
    arrived = lax.all_to_all(
        lax.all_to_all(partials, "grp", split_axis=1, concat_axis=1, tiled=True),
        "rows",
        split_axis=0,
        concat_axis=0,
        tiled=True,
    )
    item_rhs = (
        jnp.zeros((table_rows, embed_width), jnp.float32)
        .at[incoming.reshape(-1)]
        .add(arrived.reshape(-1, embed_width), mode="drop")
    )
    return (solution, item_rhs)


def solution(mesh):
    return jax.shard_map(
        on_device,
        mesh=mesh,
        in_specs=(P(("rows", "grp"), None), P(("rows", "grp"), None), P(("rows", "grp"))),
        out_specs=(P(("rows", "grp"), None), P(("rows", "grp"), None)),
        check_vma=False,
    )
```

profile of v0, /device:TPU:2, one launch (start us, length us, event | category | flops | bytes accessed | tf_op | source)
XLA Modules:
  0.0 701.0 jit_solution(2141229603027904647)
XLA Ops:
  7.2 0.9 reshape.99
  8.1 0.7 fusion.28
  8.9 5.8 sort.17
  14.7 23.0 %gather_fusion.1 = s32[4096]{0:T(1024)S(1)} fusion(s32[4096]{0:T(1024)S(1)} %get-tuple-element.108, s32[4096]{0:T(1024)S(1)} %get-tuple-element.109), kind=kCustom, calls=%fused_computation.1 | custom fusion | bytes 49152 | tf_op jit(solution)/shard_map/gather | solution.py:32
  37.8 30.3 %while.24 = (s32[]{:T(128)}, u32[257]{0:T(512)S(1)}, u32[257]{0:T(512)S(1)}, s32[4096]{0:T(1024)S(1)}, s32[]{:T(128)}, /*index=5*/s32[]{:T(128)}, s32[]{}) while((s32[]{:T(128)}, u32[257]{0:T(512)S(1)}, u32[257]{0:T(512)S(1)}, s32[4096]{0:T(1024)S(1)}, s32[]{:T(128)}, /*index=5*/s32[]{:T(128)}, s32[]{}) %tuple.47), condition=%wide.region_2.3_spmd.clone, body=%wide.region_1.2_spmd.clone.sunk | while | flops 5654 | bytes 21159 | solution.py:33
  37.8 2.2 gather_fusion
  40.1 2.2 gather_fusion
  42.5 2.2 gather_fusion
  44.8 2.2 gather_fusion
  47.1 2.2 gather_fusion
  49.4 2.2 gather_fusion
  51.8 2.2 gather_fusion
  54.1 2.2 gather_fusion
  56.4 2.2 gather_fusion
  58.7 2.2 gather_fusion
  61.1 2.2 gather_fusion
  63.4 2.2 gather_fusion
  65.7 2.2 gather_fusion
  68.1 25.9 %gather_fusion.2 = s32[4096]{0:T(1024)S(1)} fusion(s32[257]{0:T(512)S(1)} %convert_element_type.36, s32[4096]{0:T(1024)S(1)} %broadcast_clamp_fusion.1), kind=kCustom, calls=%fused_computation.2 | custom fusion | bytes 49152 | tf_op jit(solution)/shard_map/gather | solution.py:34
  94.0 15.5 %scatter_custom_fusion = s32[4096]{0:T(1024)S(1)} fusion(s32[4096]{0:T(1024)S(1)} %get-tuple-element.110, s32[4096]{0:T(1024)S(1)} %add_select_fusion.1, s32[]{:T(128)} %constant.59.clone.1), kind=kCustom, calls=%fused_computation.85 | custom fusion | bytes 16388 | tf_op jit(solution)/shard_map/scatter | solution.py:36
  109.5 15.5 %scatter_custom_fusion.1 = s32[8192]{0:T(1024)S(1)} fusion(s32[4096]{0:T(1024)S(1)} %get-tuple-element.106, s32[4096]{0:T(1024)S(1)} %get-tuple-element.107, s32[]{:T(128)} %constant.58.clone.1), kind=kCustom, calls=%fused_computation.79 | custom fusion | bytes 32772 | tf_op jit(solution)/shard_map/scatter | solution.py:38
  125.3 8.6 %all_to_all.30 = s32[8,1,1024]{2,1,0:T(1,128)S(1)} all-to-all(s32[8,1,1024]{2,1,0:T(1,128)S(1)} %reshape.212), channel_id=1, replica_groups=mesh['rows'=32,'grp'=8] {'grp'}, dimensions={0} | all-to-all | bytes 65536 | tf_op jit(solution)/shard_map/all_to_all | solution.py:42
  134.0 0.5 broadcast.142
  134.5 0.7 reduce
  135.5 21.2 %all_to_all.31 = s32[32,1,256]{2,1,0:T(1,128)S(1)} all-to-all(s32[32,1,256]{2,1,0:T(1,128)S(1)} %reshape.214), channel_id=1, replica_groups=mesh['rows'=32,'grp'=8] {'rows'}, dimensions={0} | all-to-all | bytes 65536 | tf_op jit(solution)/shard_map/all_to_all | solution.py:41
  156.7 0.7 reduce.1
  157.7 24.0 %gather_fusion.3 = bf16[8192,128]{1,0:T(8,128)(2,1)S(1)} fusion(bf16[1984,128]{1,0:T(8,128)(2,1)S(1)} %copy-done, s32[8192]{0:T(1024)S(1)} %broadcast_clamp_fusion), kind=kCustom, calls=%fused_computation.3 | custom fusion | bytes 4227072 | tf_op jit(solution)/shard_map/gather | solution.py:48
  182.2 30.0 %all_to_all.32 = bf16[32,8,32,128]{3,2,0,1:T(8,128)(2,1)S(1)} all-to-all(bf16[32,8,32,128]{3,2,0,1:T(8,128)(2,1)S(1)} %copy.16), channel_id=1, replica_groups=mesh['rows'=32,'grp'=8] {'grp'}, dimensions={1} | all-to-all | bytes 4194304 | tf_op jit(solution)/shard_map/all_to_all | solution.py:50
  212.1 2.0 copy.17
  214.1 4.0 all-to-all-start.3
  218.3 1.0 fusion.38
  219.3 49.0 %all-to-all-done.3 = bf16[32,8,32,128]{3,2,1,0:T(8,128)(2,1)S(1)} async-done(((bf16[32,8,32,128]{3,2,1,0:T(8,128)(2,1)}), bf16[32,8,32,128]{3,2,1,0:T(8,128)(2,1)S(1)}, u32[]{:S(2)}, u32[]{:S(2)}) %all-to-all-start.3) | async-done | bytes 2097184 | tf_op jit(solution)/shard_map/all_to_all | solution.py:49
  268.4 14.9 %gather_fusion.4 = bf16[4096,128]{1,0:T(8,128)(2,1)} fusion(bf16[8192,128]{1,0:T(8,128)(2,1)S(1)} %bitcast.60, s32[4096]{0:T(1024)S(1)} %get-tuple-element.105), kind=kCustom, calls=%fused_computation.4 | custom fusion | bytes 2113536 | tf_op jit(solution)/shard_map/gather | solution.py:57
  283.3 1.7 fusion.26
  285.0 1.9 fusion.24
  286.9 1.6 fusion.22
  288.5 179.1 %all-reduce.2.cloned.1.call-done = f32[128,128]{1,0:T(8,128)} async-done(((f32[128,128]{1,0:T(8,128)}), f32[128,128]{1,0:T(8,128)}) %all-reduce.2.cloned.1.call-update) | async-done | bytes 65552 | tf_op jit(solution)/shard_map/psum | solution.py:23
  467.6 1.2 multiply_reduce_fusion.3
  469.1 1.9 fusion.20
  471.5 1.1 multiply_reduce_fusion.1
  472.9 0.6 fusion.16
  474.6 12.8 %scatter_custom_fusion.2 = f32[8192,128]{1,0:T(8,128)} fusion(s32[4096]{0:T(1024)S(1)} %get-tuple-element.106, f32[4096,128]{1,0:T(8,128)S(1)} %bitcast.63, f32[]{:T(128)} %constant.71.clone.1), kind=kCustom, calls=%fused_computation.15 | custom fusion | bytes 4194308 | tf_op jit(solution)/shard_map/scatter | solution.py:82
  487.4 2.8 copy.18
  490.2 53.3 %all_to_all.33 = f32[32,8,32,128]{3,2,0,1:T(8,128)S(1)} all-to-all(f32[32,8,32,128]{3,2,0,1:T(8,128)S(1)} %copy.18), channel_id=1, replica_groups=mesh['rows'=32,'grp'=8] {'grp'}, dimensions={1} | all-to-all | bytes 8388608 | tf_op jit(solution)/shard_map/all_to_all | solution.py:86
  543.5 2.6 copy.19
  546.1 6.1 all-to-all-start.5
  552.4 96.5 %all-to-all-done.5 = f32[32,8,32,128]{3,2,1,0:T(8,128)} async-done(((f32[32,8,32,128]{3,2,1,0:T(8,128)}), f32[32,8,32,128]{3,2,1,0:T(8,128)}, u32[]{:S(2)}, u32[]{:S(2)}) %all-to-all-start.5) | async-done | bytes 4194336 | tf_op jit(solution)/shard_map/all_to_all | solution.py:85
  648.8 45.3 %scatter_custom_fusion.3 = f32[1984,128]{1,0:T(8,128)} fusion(s32[8192]{0:T(1024)S(1)} %bitcast.84, f32[8192,128]{1,0:T(8,128)} %bitcast.29, f32[]{:T(128)} %constant.71.clone.1), kind=kCustom, calls=%fused_computation.28 | custom fusion | flops 1048576 | bytes 1016320 | tf_op jit(solution)/shard_map/scatter-add | solution.py:95
  (119 shorter events, 4.4 us)
Async XLA Ops:
  7.2 150.5 %copy-start = (bf16[1984,128]{1,0:T(8,128)(2,1)S(1)}, bf16[1984,128]{1,0:T(8,128)(2,1)}, u32[]{:S(2)}) copy-start(bf16[1984,128]{1,0:T(8,128)(2,1)} %param.5) | copy-start | bytes 1523716
  214.1 54.3 %all-to-all-start.3 = ((bf16[32,8,32,128]{3,2,1,0:T(8,128)(2,1)}), bf16[32,8,32,128]{3,2,1,0:T(8,128)(2,1)S(1)}, u32[]{:S(2)}, u32[]{:S(2)}) async-start(bf16[32,8,32,128]{3,2,1,0:T(8,128)(2,1)} %copy.17), calls=%async_computation.3 | async-start | bytes 4194304 | tf_op jit(solution)/shard_map/all_to_all | solution.py:49
  218.1 249.5 %all-reduce.2.cloned.1.call-start = ((), (), s32[]{:S(2)}) async-start(), calls=%async_computation.6 | async-start | bytes 131072 | tf_op jit(solution)/shard_map/psum | solution.py:23
  268.4 18.5 %copy-start.4 = (s32[64]{0:T(128)S(1)}, s32[64]{0:T(128)}, u32[]{:S(2)}) copy-start(s32[64]{0:T(128)} %param.7) | copy-start | bytes 772
  283.3 187.8 %copy-start.1 = (bf16[4096,128]{1,0:T(8,128)(2,1)S(1)}, bf16[4096,128]{1,0:T(8,128)(2,1)}, u32[]{:S(2)}) copy-start(bf16[4096,128]{1,0:T(8,128)(2,1)} %gather_fusion.4) | copy-start | bytes 3145732
  467.6 6.4 copy-start.2
  474.5 15.7 %copy-start.3 = (f32[64,128]{1,0:T(8,128)}, f32[64,128]{1,0:T(8,128)S(1)}, u32[]{:S(2)}) copy-start(f32[64,128]{1,0:T(8,128)S(1)} %multiply_add_fusion) | copy-start | bytes 98308
  546.1 102.8 %all-to-all-start.5 = ((f32[32,8,32,128]{3,2,1,0:T(8,128)}), f32[32,8,32,128]{3,2,1,0:T(8,128)}, u32[]{:S(2)}, u32[]{:S(2)}) async-start(f32[32,8,32,128]{3,2,1,0:T(8,128)} %copy.19), calls=%async_computation.5 | async-start | bytes 8388608 | tf_op jit(solution)/shard_map/all_to_all | solution.py:85
Sparse Core Ops, SparseCore 0:
  225.0 242.5 all-reduce.1
where the time goes:
time: 702 us; the launch traced here: 701 us
  waiting for transfers between devices  325 us (46%)
  local copies, waits for them, and re-layouts  171 us (24%)
  blocking collectives  113 us (16%)
  other arithmetic  54.8 us (8%)
  between operations  14.4 us (2%)
  matrix products  12 us (2%)
  starting transfers between devices  10.4 us (1%)
    psum x1, waiting for transfers between devices, on_device(): gramian = lax.psum(local_gram, ('rows', 'grp'))  179 us
    all_to_all x1, waiting for transfers between devices, on_device(): lax.all_to_all(lax.all_to_all(partials, 'grp', split_axis=1, concat_axis=...  96.5 us
    all_to_all x1, blocking collectives, on_device(): lax.all_to_all(partials, 'grp', split_axis=1, concat_axis=1, tiled=True)  53.3 us
    all_to_all x1, waiting for transfers between devices, on_device(): lax.all_to_all(lax.all_to_all(answered, 'grp', split_axis=1, concat_axis=...  49 us
    scatter-add x1, other arithmetic, on_device(): item_rhs = jnp.zeros((table_rows, embed_width), jnp.float32).at[incoming....  45.3 us
    all_to_all x1, blocking collectives, on_device(): lax.all_to_all(answered, 'grp', split_axis=1, concat_axis=1, tiled=True)  30 us
    gather x13, local copies, waits for them, and re-layouts, on_device(): jnp.searchsorted(sorted_key, jnp.arange(devices + 1, dtype=jnp.int32), si...  29 us
    gather x1, local copies, waits for them, and re-layouts, on_device(): ranks = jnp.arange(lookups, dtype=jnp.int32) - starts[sorted_key]  25.9 us
  transfers between devices with their start and end apart: 3, of which 3 were waited for; matrix products, arithmetic and copies ran while one was open for 3% of the time, Pallas kernels for 0%

commit v1 on v0

--- a/solution.py
+++ b/solution.py
@@ -20,7 +20,7 @@
     local_gram = lax.dot_general(
         item_table, item_table, (((0,), (0,)), ((), ())), preferred_element_type=jnp.float32
     )
-    gramian = lax.psum(local_gram, ("rows", "grp"))
+    gramian = jnp.sum(lax.all_gather(local_gram, ("rows", "grp")), axis=0)
     positions = lax.broadcasted_iota(jnp.int32, (user_count, history_length), 1)
     live = positions < counts[:, None]
     weights = live.astype(jnp.float32)

time: 702 us -> 525 us (0.75)
  waiting for transfers between devices: 325 us -> 96.5 us
  blocking collectives: 113 us -> 167 us
    psum x1 -> x0, waiting for transfers between devices: 179 us -> none  [on_device(): gramian = lax.psum(local_gram, ('rows', 'grp'))]
    all_to_all x0 -> x1, blocking collectives: none -> 54.1 us  [on_device(): lax.all_to_all(lax.all_to_all(answered, 'grp', split_axis=1, concat_axis=...]
    all_to_all x1 -> x0, waiting for transfers between devices: 49 us -> none  [on_device(): lax.all_to_all(lax.all_to_all(answered, 'grp', split_axis=1, concat_axis=...]
  transfers between devices with their start and end apart: 3 -> 2, of which waited for: 3 -> 1; matrix products, arithmetic and copies ran while one was open for 3% -> 31% of each run, Pallas kernels for 0% -> 0%
where the time goes in v1:
time: 525 us; the launch traced here: 524 us
  local copies, waits for them, and re-layouts  171 us (33%)
  blocking collectives  167 us (32%)
  waiting for transfers between devices  96.5 us (18%)
  other arithmetic  61.5 us (12%)
  between operations  14.4 us (3%)
  matrix products  8.99 us (2%)
    all_to_all x1, waiting for transfers between devices, on_device(): lax.all_to_all(lax.all_to_all(partials, 'grp', split_axis=1, concat_axis=...  96.5 us
    all_to_all x1, blocking collectives, on_device(): lax.all_to_all(lax.all_to_all(answered, 'grp', split_axis=1, concat_axis=...  54.1 us
    all_to_all x1, blocking collectives, on_device(): lax.all_to_all(partials, 'grp', split_axis=1, concat_axis=1, tiled=True)  52.8 us
    scatter-add x1, other arithmetic, on_device(): item_rhs = jnp.zeros((table_rows, embed_width), jnp.float32).at[incoming....  45.3 us
    all_to_all x1, blocking collectives, on_device(): lax.all_to_all(answered, 'grp', split_axis=1, concat_axis=1, tiled=True)  30 us
    gather x13, local copies, waits for them, and re-layouts, on_device(): jnp.searchsorted(sorted_key, jnp.arange(devices + 1, dtype=jnp.int32), si...  29 us
    gather x1, local copies, waits for them, and re-layouts, on_device(): ranks = jnp.arange(lookups, dtype=jnp.int32) - starts[sorted_key]  25.9 us
    gather x2, local copies, waits for them, and re-layouts, on_device(): answered = item_table[jnp.minimum(incoming, table_rows - 1)]  24.5 us
  transfers between devices with their start and end apart: 2, of which 1 were waited for; matrix products, arithmetic and copies ran while one was open for 31% of the time, Pallas kernels for 0%

profile of v1, /device:TPU:2, one launch (start us, length us, event | category | flops | bytes accessed | tf_op | source)
XLA Modules:
  0.0 524.5 jit_solution(8467153001578466144)
XLA Ops:
  7.2 1.0 copy-done
  8.2 1.0 fusion.38
  9.2 0.8 reshape.99
  10.1 0.7 fusion.28
  10.9 5.8 %sort.17 = (s32[4096]{0:T(1024)}, s32[4096]{0:T(1024)S(1)}) sort(s32[4096]{0:T(1024)S(1)} %get-tuple-element.108, s32[4096]{0:T(1024)S(1)} %iota.18), dimensions={0}, to_apply=%region_0.0 | sort | flops 49152 | bytes 65536 | tf_op jit(solution)/shard_map/jit(argsort)/sort | solution.py:31
  16.7 23.0 %gather_fusion.1 = s32[4096]{0:T(1024)S(1)} fusion(s32[4096]{0:T(1024)S(1)} %get-tuple-element.108, s32[4096]{0:T(1024)S(1)} %get-tuple-element.109), kind=kCustom, calls=%fused_computation.1 | custom fusion | bytes 49152 | tf_op jit(solution)/shard_map/gather | solution.py:32
  39.7 30.3 %while.24 = (s32[]{:T(128)}, u32[257]{0:T(512)S(1)}, u32[257]{0:T(512)S(1)}, s32[4096]{0:T(1024)S(1)}, s32[]{:T(128)}, /*index=5*/s32[]{:T(128)}, s32[]{}) while((s32[]{:T(128)}, u32[257]{0:T(512)S(1)}, u32[257]{0:T(512)S(1)}, s32[4096]{0:T(1024)S(1)}, s32[]{:T(128)}, /*index=5*/s32[]{:T(128)}, s32[]{}) %tuple.47), condition=%wide.region_2.3_spmd.clone, body=%wide.region_1.2_spmd.clone.sunk | while | flops 5654 | bytes 21159 | solution.py:33
  39.8 2.2 gather_fusion
  42.1 2.2 gather_fusion
  44.4 2.2 gather_fusion
  46.8 2.2 gather_fusion
  49.1 2.2 gather_fusion
  51.4 2.2 gather_fusion
  53.7 2.2 gather_fusion
  56.1 2.2 gather_fusion
  58.4 2.2 gather_fusion
  60.7 2.2 gather_fusion
  63.0 2.2 gather_fusion
  65.4 2.2 gather_fusion
  67.7 2.2 gather_fusion
  70.0 25.9 %gather_fusion.2 = s32[4096]{0:T(1024)S(1)} fusion(s32[257]{0:T(512)S(1)} %convert_element_type.36, s32[4096]{0:T(1024)S(1)} %broadcast_clamp_fusion.1), kind=kCustom, calls=%fused_computation.2 | custom fusion | bytes 49152 | tf_op jit(solution)/shard_map/gather | solution.py:34
  96.0 15.5 %scatter_custom_fusion = s32[4096]{0:T(1024)S(1)} fusion(s32[4096]{0:T(1024)S(1)} %get-tuple-element.110, s32[4096]{0:T(1024)S(1)} %add_select_fusion.1, s32[]{:T(128)} %constant.59.clone.1), kind=kCustom, calls=%fused_computation.85 | custom fusion | bytes 16388 | tf_op jit(solution)/shard_map/scatter | solution.py:36
  111.5 15.5 %scatter_custom_fusion.1 = s32[8192]{0:T(1024)S(1)} fusion(s32[4096]{0:T(1024)S(1)} %get-tuple-element.106, s32[4096]{0:T(1024)S(1)} %get-tuple-element.107, s32[]{:T(128)} %constant.58.clone.1), kind=kCustom, calls=%fused_computation.79 | custom fusion | bytes 32772 | tf_op jit(solution)/shard_map/scatter | solution.py:38
  127.3 8.6 %all_to_all.30 = s32[8,1,1024]{2,1,0:T(1,128)S(1)} all-to-all(s32[8,1,1024]{2,1,0:T(1,128)S(1)} %reshape.213), channel_id=1, replica_groups=mesh['rows'=32,'grp'=8] {'grp'}, dimensions={0} | all-to-all | bytes 65536 | tf_op jit(solution)/shard_map/all_to_all | solution.py:42
  135.9 0.5 broadcast.142
  136.4 0.7 reduce
  137.5 21.2 %all_to_all.31 = s32[32,1,256]{2,1,0:T(1,128)S(1)} all-to-all(s32[32,1,256]{2,1,0:T(1,128)S(1)} %reshape.215), channel_id=1, replica_groups=mesh['rows'=32,'grp'=8] {'rows'}, dimensions={0} | all-to-all | bytes 65536 | tf_op jit(solution)/shard_map/all_to_all | solution.py:41
  158.7 0.7 reduce.1
  159.6 24.0 %gather_fusion.3 = bf16[8192,128]{1,0:T(8,128)(2,1)S(1)} fusion(bf16[1984,128]{1,0:T(8,128)(2,1)S(1)} %copy-done, s32[8192]{0:T(1024)S(1)} %broadcast_clamp_fusion), kind=kCustom, calls=%fused_computation.3 | custom fusion | bytes 4227072 | tf_op jit(solution)/shard_map/gather | solution.py:48
  183.7 0.4 copy.16
  184.1 30.0 %all_to_all.32 = bf16[32,8,32,128]{3,2,0,1:T(8,128)(2,1)S(1)} all-to-all(bf16[32,8,32,128]{3,2,0,1:T(8,128)(2,1)S(1)} %copy.16), channel_id=1, replica_groups=mesh['rows'=32,'grp'=8] {'grp'}, dimensions={1} | all-to-all | bytes 4194304 | tf_op jit(solution)/shard_map/all_to_all | solution.py:50
  214.1 0.6 copy.17
  214.7 54.1 %all_to_all.33 = bf16[32,8,32,128]{3,2,1,0:T(8,128)(2,1)S(1)} all-to-all(bf16[32,8,32,128]{3,2,1,0:T(8,128)(2,1)S(1)} %copy.17), channel_id=1, replica_groups=mesh['rows'=32,'grp'=8] {'rows'}, dimensions={0} | all-to-all | bytes 4194304 | tf_op jit(solution)/shard_map/all_to_all | solution.py:49
  268.8 14.9 %gather_fusion.4 = bf16[4096,128]{1,0:T(8,128)(2,1)} fusion(bf16[8192,128]{1,0:T(8,128)(2,1)S(1)} %bitcast.61, s32[4096]{0:T(1024)S(1)} %get-tuple-element.105), kind=kCustom, calls=%fused_computation.4 | custom fusion | bytes 2113536 | tf_op jit(solution)/shard_map/gather | solution.py:57
  283.7 1.6 fusion.26
  285.3 1.9 fusion.24
  287.2 1.6 fusion.22
  288.9 6.7 %reduce_sum.64 = f32[128,128]{1,0:T(8,128)S(1)} reduce(f32[256,128,128]{2,1,0:T(8,128)} %bitcast.62, f32[]{:T(128)} %constant.71.clone.1), dimensions={0}, to_apply=%region_6.7 | reduce | flops 4177920 | bytes 16842756 | tf_op jit(solution)/shard_map/reduce_sum | solution.py:23
  296.2 0.6 fusion.20
  296.9 0.4 fusion.18
  297.9 0.6 fusion.16
  299.6 12.8 %scatter_custom_fusion.2 = f32[8192,128]{1,0:T(8,128)} fusion(s32[4096]{0:T(1024)S(1)} %get-tuple-element.106, f32[4096,128]{1,0:T(8,128)S(1)} %bitcast.65, f32[]{:T(128)} %constant.71.clone.1), kind=kCustom, calls=%fused_computation.15 | custom fusion | bytes 4194308 | tf_op jit(solution)/shard_map/scatter | solution.py:82
  312.3 2.8 copy.18
  315.1 52.8 %all_to_all.34 = f32[32,8,32,128]{3,2,0,1:T(8,128)S(1)} all-to-all(f32[32,8,32,128]{3,2,0,1:T(8,128)S(1)} %copy.18), channel_id=1, replica_groups=mesh['rows'=32,'grp'=8] {'grp'}, dimensions={1} | all-to-all | bytes 8388608 | tf_op jit(solution)/shard_map/all_to_all | solution.py:86
  368.0 2.6 copy.19
  370.6 5.2 all-to-all-start.5
  375.9 96.5 %all-to-all-done.5 = f32[32,8,32,128]{3,2,1,0:T(8,128)} async-done(((f32[32,8,32,128]{3,2,1,0:T(8,128)}), f32[32,8,32,128]{3,2,1,0:T(8,128)}, u32[]{:S(2)}, u32[]{:S(2)}) %all-to-all-start.5) | async-done | bytes 4194336 | tf_op jit(solution)/shard_map/all_to_all | solution.py:85
  472.4 45.3 %scatter_custom_fusion.3 = f32[1984,128]{1,0:T(8,128)} fusion(s32[8192]{0:T(1024)S(1)} %bitcast.86, f32[8192,128]{1,0:T(8,128)} %bitcast.30, f32[]{:T(128)} %constant.71.clone.1), kind=kCustom, calls=%fused_computation.28 | custom fusion | flops 1048576 | bytes 1016320 | tf_op jit(solution)/shard_map/scatter-add | solution.py:95
  (117 shorter events, 4.0 us)
Async XLA Ops:
  7.2 1.0 copy-start
  7.2 281.7 %all-gather.3.cloned.1.call-start = ((), (), s32[]{:S(2)}) async-start(), calls=%async_computation.6 | async-start | bytes 16842752 | tf_op jit(solution)/shard_map/all_gather | solution.py:23
  268.8 18.4 %copy-start.3 = (s32[64]{0:T(128)S(1)}, s32[64]{0:T(128)}, u32[]{:S(2)}) copy-start(s32[64]{0:T(128)} %param.7) | copy-start | bytes 772
  288.9 7.3 %copy-start.1 = (bf16[4096,128]{1,0:T(8,128)(2,1)S(1)}, bf16[4096,128]{1,0:T(8,128)(2,1)}, u32[]{:S(2)}) copy-start(bf16[4096,128]{1,0:T(8,128)(2,1)} %gather_fusion.4) | copy-start | bytes 3145732
  299.4 15.7 %copy-start.2 = (f32[64,128]{1,0:T(8,128)}, f32[64,128]{1,0:T(8,128)S(1)}, u32[]{:S(2)}) copy-start(f32[64,128]{1,0:T(8,128)S(1)} %multiply_add_fusion) | copy-start | bytes 98308
  370.6 101.8 %all-to-all-start.5 = ((f32[32,8,32,128]{3,2,1,0:T(8,128)}), f32[32,8,32,128]{3,2,1,0:T(8,128)}, u32[]{:S(2)}, u32[]{:S(2)}) async-start(f32[32,8,32,128]{3,2,1,0:T(8,128)} %copy.19), calls=%async_computation.5 | async-start | bytes 8388608 | tf_op jit(solution)/shard_map/all_to_all | solution.py:85
Sparse Core Ops, SparseCore 0:
  12.2 127.7 all-gather.2
